TPU v7x, 256 devices: a whole 4x4x8 slice. The times are simulated.
256 devices in a mesh: var: 8 (over y, core), tok: 32 (over x, z).
Axes of the slice: x: 4, y: 4, z: 8, core: 2. Of those that a mesh axis runs over, the one named last changes fastest.
Arguments:
- patches: bfloat16 [72, 4, 4096], P('var', None, 'tok'), may hold values from -6 to 6
- slot_var: int32 [72], replicated, may hold values from -1 to 47, as said below
- patch_weight: bfloat16 [48, 4, 1024], replicated, may hold values from -3 to 3
- var_embed: bfloat16 [48, 1024], replicated, may hold values from -6 to 6
- query: bfloat16 [1024], replicated, may hold values from -16 to 16
- key_weight: bfloat16 [1024, 1024], P('tok'), may hold values from -0.1875 to 0.1875
- value_weight: bfloat16 [1024, 1024], P('tok'), may hold values from -0.1875 to 0.1875
- out_weight: bfloat16 [1024, 1024], P('tok'), may hold values from -0.1875 to 0.1875
- cotangent: bfloat16 [4096, 1024], P(('tok', 'var')), may hold values from -6 to 6
Outputs:
- aggregated: bfloat16 [4096, 1024], P(('tok', 'var'))
- patch_grad: float32 [72, 4096], P('var', 'tok')
Inputs may be any that keep to these rules, and one draw needn't show every extreme that they name: `slot_var`: slot 9 * i + j belongs to index i of var. Every variable id stands in exactly one slot; empty slots hold -1. The live slots of an index come first and hold consecutive ids, rising from index to index. Every index holds at least one and at most 9 live slots, and some index holds exactly 9.
All inputs are finite; a program needn't handle non-finite values.
Results may differ from a plain program's by a relative error of at most 0.011.
Values may be sent and summed in bfloat16 or wider, within the bound.
No kernel may reach another device: no remote copies, remote signals or barrier semaphores. Data moves between devices by JAX's collectives and lax.ppermute only.
A program may use at most 128 MiB of HBM per device.

v0:
```python
import math
import jax
import jax.numpy as jnp
from jax import lax
from jax.sharding import PartitionSpec as P

H = 16
HD = 64
score_cap = 5.0
inv_sqrt_two = 1.0 / math.sqrt(2.0)
inv_sqrt_two_pi = 1.0 / math.sqrt(2.0 * math.pi)
f32 = jnp.float32
bf16 = jnp.bfloat16


def gelu_exact(inputs):
    return 0.5 * inputs * (1.0 + lax.erf(inputs * inv_sqrt_two))


def gelu_slope(inputs):
    return (
        0.5 * (1.0 + lax.erf(inputs * inv_sqrt_two))
        + inputs * jnp.exp(-0.5 * inputs * inputs) * inv_sqrt_two_pi
    )


def live_index(slot_var, var_total):
    ids = jnp.arange(var_total, dtype=jnp.int32)
    places = jnp.arange(slot_var.shape[0], dtype=jnp.int32)
    match = slot_var[None, :] == ids[:, None]
    return jnp.sum(jnp.where(match, places[None, :], 0), axis=1)


def split(x):
    hi = x.astype(bf16)
    lo = (x - hi.astype(f32)).astype(bf16)
    return (hi, lo)


def ein(spec, a, b):
    return jnp.einsum(spec, a, b, preferred_element_type=f32)


def body(
    patches,
    slot_var,
    patch_weight,
    var_embed,
    query,
    key_weight,
    value_weight,
    out_weight,
    cotangent,
    *,
    n_var,
    n_tok
):
    var_total, pixels_per, width = patch_weight.shape
    local_slots = patches.shape[0]
    rows = key_weight.shape[0]
    tok_count = cotangent.shape[0]
    query_heads = query.reshape(H, HD).astype(f32)
    wq_rows = jnp.sum(key_weight.reshape(rows, H, HD).astype(f32) * query_heads[None], axis=2)
    wq_copies = jnp.broadcast_to(wq_rows[None], (n_tok, rows, H))
    wq_full = lax.all_to_all(wq_copies, "tok", 0, 0, tiled=True).reshape(n_tok * rows, H)
    wq_hi, wq_lo = split(wq_full)
    full = lax.all_gather(jnp.stack([value_weight, out_weight]), "tok", axis=1, tiled=True)
    value_matrix = full[0]
    out_matrix = full[1]
    slot_pixels = lax.all_to_all(patches, "var", 2, 0, tiled=True)
    live_slot = live_index(slot_var, var_total)
    pixels = jnp.take(slot_pixels, live_slot, axis=0)
    pre_act = ein("vpt,vpd->vtd", pixels, patch_weight) + var_embed.astype(f32)[:, None, :]
    embedded = gelu_exact(pre_act).astype(bf16)
    raw_scores = (
        ein("vtd,dh->tvh", embedded, wq_hi) + ein("vtd,dh->tvh", embedded, wq_lo)
    ) / math.sqrt(HD)
    squashed = jnp.tanh(raw_scores / score_cap)
    exp_scores = jnp.exp(score_cap * squashed)
    attn_f32 = exp_scores / jnp.sum(exp_scores, axis=1, keepdims=True)
    attn_bf = attn_f32.astype(bf16)
    value_heads = value_matrix.reshape(width, H, HD)
    mixed_in = ein("tvh,vtd->thd", attn_bf, embedded)
    mix_hi, mix_lo = split(mixed_in)
    pooled = (
        (ein("thd,dhj->thj", mix_hi, value_heads) + ein("thd,dhj->thj", mix_lo, value_heads))
        .astype(bf16)
        .reshape(tok_count, width)
    )
    mixed_out = jnp.dot(pooled, out_matrix, preferred_element_type=f32).astype(bf16)
    contract = (((1,), (1,)), ((), ()))
    grad_pooled = (
        lax.dot_general(cotangent, out_matrix, contract, preferred_element_type=f32)
        .astype(bf16)
        .reshape(tok_count, H, HD)
    )
    spread = ein("thj,dhj->thd", grad_pooled, value_heads)
    spread_hi, spread_lo = split(spread)
    grad_attn = ein("vtd,thd->tvh", embedded, spread_hi) + ein("vtd,thd->tvh", embedded, spread_lo)
    grad_scores = attn_f32 * (grad_attn - jnp.sum(attn_f32 * grad_attn, axis=1, keepdims=True))
    grad_raw = grad_scores * (1.0 - squashed * squashed) / math.sqrt(HD)
    raw_hi, raw_lo = split(grad_raw)
    grad_embed = (
        ein("tvh,thd->vtd", attn_bf, spread_hi)
        + ein("tvh,thd->vtd", attn_bf, spread_lo)
        + ein("tvh,dh->vtd", raw_hi, wq_hi)
        + ein("tvh,dh->vtd", raw_hi, wq_lo)
        + ein("tvh,dh->vtd", raw_lo, wq_hi)
    ).astype(bf16)
    grad_pre = grad_embed.astype(f32) * gelu_slope(pre_act)
    partial = jnp.einsum(
        "vpt,vtd->vpd", pixels.astype(f32), grad_pre, precision=lax.Precision.HIGHEST
    ).reshape(var_total, pixels_per * width)
    slots = n_var * local_slots
    cols = partial.shape[1] // n_tok
    safe = jnp.clip(slot_var, 0, var_total - 1)
    slot_rows = jnp.where((slot_var >= 0)[:, None], jnp.take(partial, safe, axis=0), 0.0)
    blocks = slot_rows.reshape(n_var, local_slots, n_tok, cols).transpose(0, 2, 1, 3)
    by_var = lax.all_to_all(blocks, "var", 0, 0, tiled=True).sum(axis=0)
    by_tok = lax.all_to_all(by_var, "tok", 0, 0, tiled=True).sum(axis=0)
    del slots
    return (mixed_out, by_tok)


def solution(mesh):
    import functools

    fn = functools.partial(body, n_var=mesh.shape["var"], n_tok=mesh.shape["tok"])
    return jax.shard_map(
        fn,
        mesh=mesh,
        in_specs=(
            P("var", None, "tok"),
            P(),
            P(),
            P(),
            P(),
            P("tok", None),
            P("tok", None),
            P("tok", None),
            P(("tok", "var"), None),
        ),
        out_specs=(P(("tok", "var"), None), P("var", "tok")),
        check_vma=False,
    )
```

profile of v0, /device:TPU:32, one launch (start us, length us, event | category | flops | bytes accessed | tf_op | source)
XLA Modules:
  0.0 189.6 jit_solution(7815867198240021874)
XLA Ops:
  10.5 4.5 %all-to-all-start.1 = ((bf16[8,2,288]{2,1,0:T(2,128)(2,1)}), bf16[8,2,288]{2,1,0:T(2,128)(2,1)S(1)}, u32[]{:S(2)}, u32[]{:S(2)}) async-start(bf16[8,2,288]{2,1,0:T(2,128)(2,1)} %reshape.93), calls=%async_computation.1 | async-start | bytes 24576 | tf_op jit(solution)/shard_map/all_to_all | solution.py:70
  20.9 11.2 %all-to-all-start = ((f32[32,1,512]{2,1,0:T(1,128)}), f32[32,1,512]{2,1,0:T(1,128)S(1)}, u32[]{:S(2)}, u32[]{:S(2)}) async-start(f32[32,1,512]{2,1,0:T(1,128)} %reshape.95), calls=%async_computation | async-start | bytes 131072 | tf_op jit(solution)/shard_map/all_to_all | solution.py:65
  33.4 2.9 %multiply_convert_fusion = (bf16[48,16,1024]{2,1,0:T(8,128)(2,1)S(1)}, f32[48,16,1024]{2,1,0:T(8,128)}) fusion(f32[48,1024]{1,0:T(8,128)S(1)} %convert_element_type.88, bf16[48,4,1024]{2,1,0:T(4,128)(2,1)S(1)} %copy-done, bf16[48,4,16]{2,1,0:T(4,128)(2,1)S(1)} %gather_fusion, pred[48]{0:T(512)(128)(4,1)S(1)} %compare_and_fusion.1), kind=kOutput, calls=%fused_computation.17 | convolution fusion | flops 11013120 | bytes 5314608 | tf_op jit(solution)/shard_map/vpt,vpd->vtd/dot_general | solution.py:41
  36.4 5.1 %all-to-all-done = f32[32,1,512]{2,1,0:T(1,128)S(1)} async-done(((f32[32,1,512]{2,1,0:T(1,128)}), f32[32,1,512]{2,1,0:T(1,128)S(1)}, u32[]{:S(2)}, u32[]{:S(2)}) %all-to-all-start) | async-done | bytes 65568 | tf_op jit(solution)/shard_map/all_to_all | solution.py:65
  46.6 48.1 %all-gather.2.cloned.1.call-done = bf16[2,1024,1024]{2,1,0:T(8,128)(2,1)} async-done(((bf16[2,32,1024]{2,1,0:T(8,128)(2,1)}), bf16[2,1024,1024]{2,1,0:T(8,128)(2,1)}) %all-gather.2.cloned.1.call-update) | async-done | bytes 4194320 | tf_op jit(solution)/shard_map/all_gather | solution.py:67
  94.7 3.1 %slice.12 = bf16[1,1024,1024]{2,1,0:T(8,128)(2,1)} slice(bf16[2,1024,1024]{2,1,0:T(8,128)(2,1)} %all-gather.2.cloned.1.call-done), slice={[0:1], [0:1024], [0:1024]} | slice | bytes 4194304 | tf_op jit(solution)/shard_map/slice | solution.py:68
  97.8 3.0 %copy.107 = bf16[1,1024,1024]{1,2,0:T(8,128)(2,1)S(1)} copy(bf16[1,1024,1024]{2,1,0:T(8,128)(2,1)} %slice.12) | data formatting | bytes 4194304 | tf_op jit(solution)/shard_map/slice | solution.py:68
  100.9 2.2 %fusion.28 = bf16[16,1024]{1,0:T(8,128)(2,1)S(1)} fusion(bf16[16,1024]{1,0:T(8,128)(2,1)S(1)} %copy-done.20, bf16[2,1024,1024]{2,1,0:T(8,128)(2,1)} %all-gather.2.cloned.1.call-done), kind=kOutput, calls=%fused_computation.42 | convolution fusion | flops 33570816 | bytes 2162688 | tf_op jit(solution)/shard_map/dot_general | solution.py:93
  106.8 2.6 %convolution_add_fusion.2 = f32[16,48,16]{1,2,0:T(8,128)S(1)} fusion(f32[16,48,16]{1,2,0:T(8,128)S(1)} %fusion.30, bf16[48,16,1024]{2,1,0:T(8,128)(2,1)S(1)} %copy-done.2, bf16[16,16,1024]{2,0,1:T(8,128)(2,1)S(1)} %get-tuple-element.8), kind=kOutput, calls=%fused_computation.37 | convolution fusion | flops 25178112 | bytes 2195456 | tf_op jit(solution)/shard_map/vtd,thd->tvh/dot_general | solution.py:41
  109.4 1.9 %subtract_convert_fusion.2 = (bf16[16,48,16]{1,2,0:T(8,128)(2,1)}, bf16[16,48,16]{1,2,0:T(8,128)(2,1)}) fusion(f32[16,48,16]{1,0,2:T(8,128)S(1)} %copy-done.15, f32[16,48,16]{1,2,0:T(8,128)S(1)} %convolution_add_fusion.2, f32[16,16]{1,0:T(8,128)S(1)} %get-tuple-element.13), kind=kOutput, calls=%fused_computation.67 | output fusion | flops 184623 | bytes 148480 | tf_op jit(solution)/shard_map/sub | solution.py:100
  111.3 1.7 copy.128
  113.0 3.3 %fusion.56 = f32[1024,16,48]{0,1,2:T(8,128)} fusion(bf16[16,48,16]{2,0,1:T(8,128)(2,1)} %copy.128, f32[1024,16]{0,1:T(8,128)} %copy-done.5), kind=kOutput, calls=%fused_computation.84 | convolution fusion | flops 25231360 | bytes 3235840 | tf_op jit(solution)/shard_map/tvh,dh->vtd/dot_general | solution.py:41
  116.4 2.3 %fusion.50 = f32[1024,16,48]{0,1,2:T(8,128)} fusion(bf16[16,48,16]{2,0,1:T(8,128)(2,1)S(1)} %copy-done.4, f32[1024,16]{0,1:T(8,128)S(1)} %copy-done.6), kind=kOutput, calls=%fused_computation.76 | convolution fusion | flops 25182208 | bytes 3235840 | tf_op jit(solution)/shard_map/tvh,dh->vtd/dot_general | solution.py:41
  118.7 2.2 %fusion.41 = f32[16,1024,48]{1,2,0:T(8,128)} fusion(bf16[16,48,16]{1,2,0:T(8,128)(2,1)S(1)} %copy-done.8, bf16[16,16,1024]{2,0,1:T(8,128)(2,1)S(1)} %get-tuple-element.8), kind=kOutput, calls=%fused_computation.57 | convolution fusion | flops 25165824 | bytes 3694592 | tf_op jit(solution)/shard_map/tvh,thd->vtd/dot_general | solution.py:41
  120.9 2.3 %fusion.44 = f32[16,1024,48]{1,2,0:T(8,128)} fusion(bf16[16,48,16]{1,2,0:T(8,128)(2,1)S(1)} %copy-done.8, bf16[16,16,1024]{2,0,1:T(8,128)(2,1)S(1)} %get-tuple-element.9), kind=kOutput, calls=%fused_computation.60 | convolution fusion | flops 25165824 | bytes 3694592 | tf_op jit(solution)/shard_map/tvh,thd->vtd/dot_general | solution.py:41
  123.4 8.5 %fusion.8 = bf16[48,16,1024]{2,1,0:T(8,128)(2,1)S(1)} fusion(f32[1024,16,48]{0,1,2:T(8,128)} %fusion.56, f32[1024,16,48]{0,1,2:T(8,128)} %fusion.50, f32[16,1024,48]{1,2,0:T(8,128)} %fusion.41, f32[16,1024,48]{1,2,0:T(8,128)} %fusion.44, bf16[16,48,16]{2,0,1:T(8,128)(2,1)S(1)} %copy.130, f32[1024,16]{0,1:T(8,128)S(1)} %copy-done.7), kind=kOutput, calls=%fused_computation.11 | convolution fusion | flops 29114368 | bytes 14245888 | tf_op jit(solution)/shard_map/tvh,dh->vtd/dot_general | solution.py:41
  131.9 3.2 %fusion.6 = f32[48,4,1024]{2,1,0:T(4,128)S(1)} fusion(bf16[48,16,1024]{2,1,0:T(8,128)(2,1)S(1)} %fusion.8, f32[48,16,1024]{2,1,0:T(8,128)S(1)} %copy-done.3, f32[48,1024]{1,0:T(8,128)S(1)} %copy-done.11, bf16[48,4,16]{2,1,0:T(4,128)(2,1)S(1)} %copy-done.13, pred[48]{0:T(512)(128)(4,1)S(1)} %copy-done.19), kind=kOutput, calls=%fused_computation.9 | convolution fusion | flops 46402560 | bytes 5707824 | tf_op jit(solution)/shard_map/vpt,vtd->vpd/dot_general | solution.py:111
  135.6 2.0 %gather_fusion.1 = f32[72,4096]{1,0:T(8,128)} fusion(f32[48,4096]{1,0:T(8,128)S(1)} %bitcast.98, s32[1024]{0:T(1024)S(1)} %pad_clamp_fusion), kind=kCustom, calls=%fused_computation.1 | custom fusion | bytes 2359584 | tf_op jit(solution)/shard_map/jit(_take)/gather | solution.py:117
  140.4 4.3 %all-to-all-start.2 = ((f32[8,32,9,128]{3,1,2,0:T(8,128)}), f32[8,32,9,128]{3,1,2,0:T(8,128)}, u32[]{:S(2)}, u32[]{:S(2)}) async-start(f32[8,32,9,128]{3,1,2,0:T(8,128)} %select_bitcast_fusion), calls=%async_computation.2 | async-start | bytes 2359296 | tf_op jit(solution)/shard_map/all_to_all | solution.py:119
  144.7 3.2 %subtract_convert_fusion.1 = (bf16[16,16,1024]{2,1,0:T(8,128)(2,1)S(1)}, bf16[16,16,1024]{2,1,0:T(8,128)(2,1)S(1)}) fusion(bf16[16,48,16]{1,2,0:T(8,128)(2,1)S(1)} %copy-done.9, bf16[48,16,1024]{2,1,0:T(8,128)(2,1)} %copy-done.1), kind=kOutput, calls=%fused_computation.44 | convolution fusion | flops 26214400 | bytes 2646016 | tf_op jit(solution)/shard_map/tvh,vtd->thd/dot_general | solution.py:41
  148.5 13.6 %all-to-all-done.2 = f32[8,32,9,128]{3,1,2,0:T(8,128)} async-done(((f32[8,32,9,128]{3,1,2,0:T(8,128)}), f32[8,32,9,128]{3,1,2,0:T(8,128)}, u32[]{:S(2)}, u32[]{:S(2)}) %all-to-all-start.2) | async-done | bytes 1179680 | tf_op jit(solution)/shard_map/all_to_all | solution.py:119
  164.3 5.8 %all-to-all-start.3 = ((f32[32,9,128]{2,1,0:T(8,128)}), f32[32,9,128]{2,1,0:T(8,128)S(1)}, u32[]{:S(2)}, u32[]{:S(2)}) async-start(f32[32,9,128]{2,1,0:T(8,128)} %copy.131), calls=%async_computation.3 | async-start | bytes 524288 | tf_op jit(solution)/shard_map/all_to_all | solution.py:120
  170.9 2.6 %fusion.26 = bf16[16,1024]{1,0:T(8,128)(2,1)} fusion(bf16[16,1024]{1,0:T(8,128)(2,1)S(1)} %reshape.69, bf16[2,1024,1024]{2,1,0:T(8,128)(2,1)} %all-gather.2.cloned.1.call-done), kind=kOutput, calls=%fused_computation.40 | convolution fusion | flops 33570816 | bytes 2162688 | tf_op jit(solution)/shard_map/dot_general | solution.py:90
  173.5 8.6 %all-to-all-done.3 = f32[32,9,128]{2,1,0:T(8,128)S(1)} async-done(((f32[32,9,128]{2,1,0:T(8,128)}), f32[32,9,128]{2,1,0:T(8,128)S(1)}, u32[]{:S(2)}, u32[]{:S(2)}) %all-to-all-start.3) | async-done | bytes 147488 | tf_op jit(solution)/shard_map/all_to_all | solution.py:120
  (89 shorter events, 27.0 us)
Async XLA Ops:
  7.2 26.2 %copy-start = (bf16[48,4,1024]{2,1,0:T(4,128)(2,1)S(1)}, bf16[48,4,1024]{2,1,0:T(4,128)(2,1)}, u32[]{:S(2)}) copy-start(bf16[48,4,1024]{2,1,0:T(4,128)(2,1)} %param.11) | copy-start | bytes 1179652
  7.2 87.5 %all-gather.2.cloned.1.call-start = ((), (), s32[]{:S(2)}) async-start(), calls=%async_computation.4 | async-start | bytes 4325376 | tf_op jit(solution)/shard_map/all_gather | solution.py:67
  10.5 10.4 %all-to-all-start.1 = ((bf16[8,2,288]{2,1,0:T(2,128)(2,1)}), bf16[8,2,288]{2,1,0:T(2,128)(2,1)S(1)}, u32[]{:S(2)}, u32[]{:S(2)}) async-start(bf16[8,2,288]{2,1,0:T(2,128)(2,1)} %reshape.93), calls=%async_computation.1 | async-start | bytes 24576 | tf_op jit(solution)/shard_map/all_to_all | solution.py:70
  17.7 18.6 %copy-start.18 = (pred[48]{0:T(512)(128)(4,1)}, pred[48]{0:T(512)(128)(4,1)S(1)}, u32[]{:S(2)}) copy-start(pred[48]{0:T(512)(128)(4,1)S(1)} %compare_and_fusion.1) | copy-start | bytes 148
  19.3 17.0 %copy-start.10 = (f32[48,1024]{1,0:T(8,128)}, f32[48,1024]{1,0:T(8,128)S(1)}, u32[]{:S(2)}) copy-start(f32[48,1024]{1,0:T(8,128)S(1)} %convert_element_type.88) | copy-start | bytes 589828
  20.9 20.6 %all-to-all-start = ((f32[32,1,512]{2,1,0:T(1,128)}), f32[32,1,512]{2,1,0:T(1,128)S(1)}, u32[]{:S(2)}, u32[]{:S(2)}) async-start(f32[32,1,512]{2,1,0:T(1,128)} %reshape.95), calls=%async_computation | async-start | bytes 131072 | tf_op jit(solution)/shard_map/all_to_all | solution.py:65
  33.4 8.0 %copy-start.12 = (bf16[48,4,16]{2,1,0:T(4,128)(2,1)}, bf16[48,4,16]{2,1,0:T(4,128)(2,1)S(1)}, u32[]{:S(2)}) copy-start(bf16[48,4,16]{2,1,0:T(4,128)(2,1)S(1)} %gather_fusion) | copy-start | bytes 18436
  36.4 58.3 %copy-start.1 = (bf16[48,16,1024]{2,1,0:T(8,128)(2,1)}, bf16[48,16,1024]{2,1,0:T(8,128)(2,1)S(1)}, u32[]{:S(2)}) copy-start(bf16[48,16,1024]{2,1,0:T(8,128)(2,1)S(1)} %get-tuple-element.11) | copy-start | bytes 4718596
  43.1 51.6 %copy-start.5 = (f32[1024,16]{0,1:T(8,128)}, f32[1024,16]{0,1:T(8,128)S(1)}, u32[]{:S(2)}) copy-start(f32[1024,16]{0,1:T(8,128)S(1)} %reshape.68) | copy-start | bytes 196612
  46.6 54.3 %copy-start.20 = (bf16[16,1024]{1,0:T(8,128)(2,1)S(1)}, bf16[16,1024]{1,0:T(8,128)(2,1)}, u32[]{:S(2)}) copy-start(bf16[16,1024]{1,0:T(8,128)(2,1)} %param.17) | copy-start | bytes 98308
  105.2 4.2 %copy-start.15 = (f32[16,48,16]{1,0,2:T(8,128)S(1)}, f32[16,48,16]{1,0,2:T(8,128)}, u32[]{:S(2)}) copy-start(f32[16,48,16]{1,0,2:T(8,128)} %copy-done.14) | copy-start | bytes 147460
  113.0 3.3 %copy-start.4 = (bf16[16,48,16]{2,0,1:T(8,128)(2,1)S(1)}, bf16[16,48,16]{2,0,1:T(8,128)(2,1)}, u32[]{:S(2)}) copy-start(bf16[16,48,16]{2,0,1:T(8,128)(2,1)} %copy.128) | copy-start | bytes 73732
  113.0 3.3 %copy-start.6 = (f32[1024,16]{0,1:T(8,128)S(1)}, f32[1024,16]{0,1:T(8,128)}, u32[]{:S(2)}) copy-start(f32[1024,16]{0,1:T(8,128)} %copy-done.5) | copy-start | bytes 196612
  113.0 5.6 %copy-start.8 = (bf16[16,48,16]{1,2,0:T(8,128)(2,1)S(1)}, bf16[16,48,16]{1,2,0:T(8,128)(2,1)}, u32[]{:S(2)}) copy-start(bf16[16,48,16]{1,2,0:T(8,128)(2,1)} %fusion.59) | copy-start | bytes 73732
  120.9 2.3 %copy-start.16 = (bf16[16,48,16]{1,2,0:T(8,128)(2,1)S(1)}, bf16[16,48,16]{1,2,0:T(8,128)(2,1)}, u32[]{:S(2)}) copy-start(bf16[16,48,16]{1,2,0:T(8,128)(2,1)} %get-tuple-element.4) | copy-start | bytes 73732
  120.9 2.5 %copy-start.7 = (f32[1024,16]{0,1:T(8,128)S(1)}, f32[1024,16]{0,1:T(8,128)}, u32[]{:S(2)}) copy-start(f32[1024,16]{0,1:T(8,128)} %copy-done.5) | copy-start | bytes 196612
  123.4 8.5 %copy-start.3 = (f32[48,16,1024]{2,1,0:T(8,128)S(1)}, f32[48,16,1024]{2,1,0:T(8,128)}, u32[]{:S(2)}) copy-start(f32[48,16,1024]{2,1,0:T(8,128)} %get-tuple-element.12) | copy-start | bytes 9437188
  123.4 8.5 %copy-start.11 = (f32[48,1024]{1,0:T(8,128)S(1)}, f32[48,1024]{1,0:T(8,128)}, u32[]{:S(2)}) copy-start(f32[48,1024]{1,0:T(8,128)} %copy-done.10) | copy-start | bytes 589828
  123.4 8.5 %copy-start.13 = (bf16[48,4,16]{2,1,0:T(4,128)(2,1)S(1)}, bf16[48,4,16]{2,1,0:T(4,128)(2,1)}, u32[]{:S(2)}) copy-start(bf16[48,4,16]{2,1,0:T(4,128)(2,1)} %copy-done.12) | copy-start | bytes 18436
  123.4 8.5 %copy-start.19 = (pred[48]{0:T(512)(128)(4,1)S(1)}, pred[48]{0:T(512)(128)(4,1)}, u32[]{:S(2)}) copy-start(pred[48]{0:T(512)(128)(4,1)} %copy-done.18) | copy-start | bytes 148
  135.6 3.5 %copy-start.17 = (pred[8,9]{1,0:T(8,128)(4,1)S(1)}, pred[8,9]{1,0:T(8,128)(4,1)}, u32[]{:S(2)}) copy-start(pred[8,9]{1,0:T(8,128)(4,1)} %broadcast_in_dim.69) | copy-start | bytes 220
  137.6 7.1 %copy-start.9 = (bf16[16,48,16]{1,2,0:T(8,128)(2,1)S(1)}, bf16[16,48,16]{1,2,0:T(8,128)(2,1)}, u32[]{:S(2)}) copy-start(bf16[16,48,16]{1,2,0:T(8,128)(2,1)} %fusion.59) | copy-start | bytes 73732
  140.4 21.7 %all-to-all-start.2 = ((f32[8,32,9,128]{3,1,2,0:T(8,128)}), f32[8,32,9,128]{3,1,2,0:T(8,128)}, u32[]{:S(2)}, u32[]{:S(2)}) async-start(f32[8,32,9,128]{3,1,2,0:T(8,128)} %select_bitcast_fusion), calls=%async_computation.2 | async-start | bytes 2359296 | tf_op jit(solution)/shard_map/all_to_all | solution.py:119
  164.3 17.8 %all-to-all-start.3 = ((f32[32,9,128]{2,1,0:T(8,128)}), f32[32,9,128]{2,1,0:T(8,128)S(1)}, u32[]{:S(2)}, u32[]{:S(2)}) async-start(f32[32,9,128]{2,1,0:T(8,128)} %copy.131), calls=%async_computation.3 | async-start | bytes 524288 | tf_op jit(solution)/shard_map/all_to_all | solution.py:120
  (2 other events, 2.1 us)
Sparse Core Ops, SparseCore 0:
  10.6 84.0 all-gather.1
where the time goes:
time: 190 us
  waiting for transfers between devices  75.3 us (40%)
  matrix products  41.6 us (22%)
  starting transfers between devices  25.8 us (14%)
  local copies, waits for them, and re-layouts  21.7 us (11%)
  between operations  14.4 us (8%)
  other arithmetic  10.8 us (6%)
    all_gather x1, waiting for transfers between devices, body(): lax.all_gather(jnp.stack([value_weight, out_weight]), 'tok', axis=1, tile...  48.1 us
    dot_general x14, matrix products, ein(): return jnp.einsum(spec, a, b, preferred_element_type=f32)  33.6 us
    all_to_all x1, waiting for transfers between devices, body(): by_var = lax.all_to_all(blocks, 'var', 0, 0, tiled=True).sum(axis=0)  13.6 us
    all_to_all x1, starting transfers between devices, body(): lax.all_to_all(wq_copies, 'tok', 0, 0, tiled=True).reshape(n_tok * rows, H)  11.2 us
    all_to_all x1, waiting for transfers between devices, body(): by_tok = lax.all_to_all(by_var, 'tok', 0, 0, tiled=True).sum(axis=0)  8.57 us
    slice x2, local copies, waits for them, and re-layouts, body(): value_matrix = full[0]  6.18 us
    all_to_all x1, starting transfers between devices, body(): by_tok = lax.all_to_all(by_var, 'tok', 0, 0, tiled=True).sum(axis=0)  5.8 us
    unnamed x50, local copies, waits for them, and re-layouts  5.65 us
  transfers between devices with their start and end apart: 5, of which 4 were waited for; matrix products, arithmetic and copies ran while one was open for 12% of the time, Pallas kernels for 0%

commit v1 on v0

--- a/solution.py
+++ b/solution.py
@@ -67,7 +67,10 @@
     full = lax.all_gather(jnp.stack([value_weight, out_weight]), "tok", axis=1, tiled=True)
     value_matrix = full[0]
     out_matrix = full[1]
-    slot_pixels = lax.all_to_all(patches, "var", 2, 0, tiled=True)
+    slot_pixels = jnp.concatenate(
+        lax.all_to_all(jnp.stack(jnp.split(patches, lax.axis_size("var"), axis=2)), "var", 0, 0),
+        axis=0,
+    )
     live_slot = live_index(slot_var, var_total)
     pixels = jnp.take(slot_pixels, live_slot, axis=0)
     pre_act = ein("vpt,vpd->vtd", pixels, patch_weight) + var_embed.astype(f32)[:, None, :]

time: 190 us -> 191 us (level)
  waiting for transfers between devices: 75.3 us -> 70.6 us
  local copies, waits for them, and re-layouts: 21.7 us -> 26.4 us
    all_gather x1, waiting for transfers between devices: 48.1 us -> 42.5 us  [body(): lax.all_gather(jnp.stack([value_weight, out_weight]), 'tok', axis=1, tile...]
    unnamed x50 -> x56, local copies, waits for them, and re-layouts: 5.65 us -> 9.95 us
  transfers between devices with their start and end apart: 5 -> 5, of which waited for: 4 -> 4; matrix products, arithmetic and copies ran while one was open for 12% -> 15% of each run, Pallas kernels for 0% -> 0%
where the time goes in v1:
time: 191 us; the launch traced here: 190 us
  waiting for transfers between devices  70.6 us (37%)
  matrix products  41.6 us (22%)
  local copies, waits for them, and re-layouts  26.4 us (14%)
  starting transfers between devices  25.8 us (14%)
  between operations  14.4 us (8%)
  other arithmetic  10.8 us (6%)
    all_gather x1, waiting for transfers between devices, body(): lax.all_gather(jnp.stack([value_weight, out_weight]), 'tok', axis=1, tile...  42.5 us
    dot_general x14, matrix products, ein(): return jnp.einsum(spec, a, b, preferred_element_type=f32)  33.6 us
    all_to_all x1, waiting for transfers between devices, body(): by_var = lax.all_to_all(blocks, 'var', 0, 0, tiled=True).sum(axis=0)  13.6 us
    all_to_all x1, starting transfers between devices, body(): lax.all_to_all(wq_copies, 'tok', 0, 0, tiled=True).reshape(n_tok * rows, H)  11.2 us
    unnamed x56, local copies, waits for them, and re-layouts  9.95 us
    all_to_all x1, waiting for transfers between devices, body(): by_tok = lax.all_to_all(by_var, 'tok', 0, 0, tiled=True).sum(axis=0)  8.57 us
    slice x2, local copies, waits for them, and re-layouts, body(): value_matrix = full[0]  6.18 us
    all_to_all x1, waiting for transfers between devices, body(): lax.all_to_all(wq_copies, 'tok', 0, 0, tiled=True).reshape(n_tok * rows, H)  5.96 us
  transfers between devices with their start and end apart: 5, of which 4 were waited for; matrix products, arithmetic and copies ran while one was open for 15% of the time, Pallas kernels for 0%

profile of v1, /device:TPU:32, one launch (start us, length us, event | category | flops | bytes accessed | tf_op | source)
XLA Modules:
  0.0 189.6 jit_solution(7799157490378960787)
XLA Ops:
  15.8 4.5 %all-to-all-start.1 = ((bf16[8,2,288]{2,1,0:T(2,128)(2,1)}), bf16[8,2,288]{2,1,0:T(2,128)(2,1)S(1)}, u32[]{:S(2)}, u32[]{:S(2)}) async-start(bf16[8,2,288]{2,1,0:T(2,128)(2,1)} %reshape.97), calls=%async_computation.1 | async-start | bytes 24576 | tf_op jit(solution)/shard_map/all_to_all | solution.py:71
  26.1 11.2 %all-to-all-start = ((f32[32,1,512]{2,1,0:T(1,128)}), f32[32,1,512]{2,1,0:T(1,128)S(1)}, u32[]{:S(2)}, u32[]{:S(2)}) async-start(f32[32,1,512]{2,1,0:T(1,128)} %reshape.99), calls=%async_computation | async-start | bytes 131072 | tf_op jit(solution)/shard_map/all_to_all | solution.py:65
  38.1 2.9 %multiply_convert_fusion = (bf16[48,16,1024]{2,1,0:T(8,128)(2,1)S(1)}, f32[48,16,1024]{2,1,0:T(8,128)}) fusion(f32[48,1024]{1,0:T(8,128)S(1)} %convert_element_type.88, bf16[48,4,1024]{2,1,0:T(4,128)(2,1)S(1)} %copy-done, bf16[48,4,16]{2,1,0:T(4,128)(2,1)S(1)} %gather_fusion, pred[48]{0:T(512)(128)(4,1)S(1)} %compare_and_fusion.1), kind=kOutput, calls=%fused_computation.17 | convolution fusion | flops 11013120 | bytes 5314608 | tf_op jit(solution)/shard_map/vpt,vpd->vtd/dot_general | solution.py:41
  41.1 6.0 %all-to-all-done = f32[32,1,512]{2,1,0:T(1,128)S(1)} async-done(((f32[32,1,512]{2,1,0:T(1,128)}), f32[32,1,512]{2,1,0:T(1,128)S(1)}, u32[]{:S(2)}, u32[]{:S(2)}) %all-to-all-start) | async-done | bytes 65568 | tf_op jit(solution)/shard_map/all_to_all | solution.py:65
  52.2 42.5 %all-gather.2.cloned.1.call-done = bf16[2,1024,1024]{2,1,0:T(8,128)(2,1)} async-done(((bf16[2,32,1024]{2,1,0:T(8,128)(2,1)}), bf16[2,1024,1024]{2,1,0:T(8,128)(2,1)}) %all-gather.2.cloned.1.call-update) | async-done | bytes 4194320 | tf_op jit(solution)/shard_map/all_gather | solution.py:67
  94.7 3.1 %slice.12 = bf16[1,1024,1024]{2,1,0:T(8,128)(2,1)} slice(bf16[2,1024,1024]{2,1,0:T(8,128)(2,1)} %all-gather.2.cloned.1.call-done), slice={[0:1], [0:1024], [0:1024]} | slice | bytes 4194304 | tf_op jit(solution)/shard_map/slice | solution.py:68
  97.8 3.0 %copy.77 = bf16[1,1024,1024]{1,2,0:T(8,128)(2,1)S(1)} copy(bf16[1,1024,1024]{2,1,0:T(8,128)(2,1)} %slice.12) | data formatting | bytes 4194304 | tf_op jit(solution)/shard_map/slice | solution.py:68
  100.9 2.2 %fusion.28 = bf16[16,1024]{1,0:T(8,128)(2,1)S(1)} fusion(bf16[16,1024]{1,0:T(8,128)(2,1)S(1)} %copy-done.20, bf16[2,1024,1024]{2,1,0:T(8,128)(2,1)} %all-gather.2.cloned.1.call-done), kind=kOutput, calls=%fused_computation.42 | convolution fusion | flops 33570816 | bytes 2162688 | tf_op jit(solution)/shard_map/dot_general | solution.py:96
  106.8 2.6 %convolution_add_fusion.2 = f32[16,48,16]{1,2,0:T(8,128)S(1)} fusion(f32[16,48,16]{1,2,0:T(8,128)S(1)} %fusion.30, bf16[48,16,1024]{2,1,0:T(8,128)(2,1)S(1)} %copy-done.2, bf16[16,16,1024]{2,0,1:T(8,128)(2,1)S(1)} %get-tuple-element.8), kind=kOutput, calls=%fused_computation.37 | convolution fusion | flops 25178112 | bytes 2195456 | tf_op jit(solution)/shard_map/vtd,thd->tvh/dot_general | solution.py:41
  109.4 1.9 %subtract_convert_fusion.2 = (bf16[16,48,16]{1,2,0:T(8,128)(2,1)}, bf16[16,48,16]{1,2,0:T(8,128)(2,1)}) fusion(f32[16,48,16]{1,0,2:T(8,128)S(1)} %copy-done.15, f32[16,48,16]{1,2,0:T(8,128)S(1)} %convolution_add_fusion.2, f32[16,16]{1,0:T(8,128)S(1)} %get-tuple-element.13), kind=kOutput, calls=%fused_computation.66 | output fusion | flops 184623 | bytes 148480 | tf_op jit(solution)/shard_map/sub | solution.py:103
  111.3 1.7 copy.95
  113.0 3.3 %fusion.56 = f32[1024,16,48]{0,1,2:T(8,128)} fusion(bf16[16,48,16]{2,0,1:T(8,128)(2,1)} %copy.95, f32[1024,16]{0,1:T(8,128)} %copy-done.5), kind=kOutput, calls=%fused_computation.91 | convolution fusion | flops 25231360 | bytes 3235840 | tf_op jit(solution)/shard_map/tvh,dh->vtd/dot_general | solution.py:41
  116.3 2.3 %fusion.50 = f32[1024,16,48]{0,1,2:T(8,128)} fusion(bf16[16,48,16]{2,0,1:T(8,128)(2,1)S(1)} %copy-done.4, f32[1024,16]{0,1:T(8,128)S(1)} %copy-done.6), kind=kOutput, calls=%fused_computation.75 | convolution fusion | flops 25182208 | bytes 3235840 | tf_op jit(solution)/shard_map/tvh,dh->vtd/dot_general | solution.py:41
  118.7 2.2 %fusion.41 = f32[16,1024,48]{1,2,0:T(8,128)} fusion(bf16[16,48,16]{1,2,0:T(8,128)(2,1)S(1)} %copy-done.8, bf16[16,16,1024]{2,0,1:T(8,128)(2,1)S(1)} %get-tuple-element.8), kind=kOutput, calls=%fused_computation.57 | convolution fusion | flops 25165824 | bytes 3694592 | tf_op jit(solution)/shard_map/tvh,thd->vtd/dot_general | solution.py:41
  120.9 2.3 %fusion.44 = f32[16,1024,48]{1,2,0:T(8,128)} fusion(bf16[16,48,16]{1,2,0:T(8,128)(2,1)S(1)} %copy-done.8, bf16[16,16,1024]{2,0,1:T(8,128)(2,1)S(1)} %get-tuple-element.9), kind=kOutput, calls=%fused_computation.60 | convolution fusion | flops 25165824 | bytes 3694592 | tf_op jit(solution)/shard_map/tvh,thd->vtd/dot_general | solution.py:41
  123.4 8.5 %fusion.8 = bf16[48,16,1024]{2,1,0:T(8,128)(2,1)S(1)} fusion(f32[1024,16,48]{0,1,2:T(8,128)} %fusion.56, f32[1024,16,48]{0,1,2:T(8,128)} %fusion.50, f32[16,1024,48]{1,2,0:T(8,128)} %fusion.41, f32[16,1024,48]{1,2,0:T(8,128)} %fusion.44, bf16[16,48,16]{2,0,1:T(8,128)(2,1)S(1)} %copy.97, f32[1024,16]{0,1:T(8,128)S(1)} %copy-done.7), kind=kOutput, calls=%fused_computation.11 | convolution fusion | flops 29114368 | bytes 14245888 | tf_op jit(solution)/shard_map/tvh,dh->vtd/dot_general | solution.py:41
  132.0 3.2 %fusion.6 = f32[48,4,1024]{2,1,0:T(4,128)S(1)} fusion(bf16[48,16,1024]{2,1,0:T(8,128)(2,1)S(1)} %fusion.8, f32[48,16,1024]{2,1,0:T(8,128)S(1)} %copy-done.3, f32[48,1024]{1,0:T(8,128)S(1)} %copy-done.11, bf16[48,4,16]{2,1,0:T(4,128)(2,1)S(1)} %copy-done.13, pred[48]{0:T(512)(128)(4,1)S(1)} %copy-done.19), kind=kOutput, calls=%fused_computation.9 | convolution fusion | flops 46402560 | bytes 5707824 | tf_op jit(solution)/shard_map/vpt,vtd->vpd/dot_general | solution.py:114
  135.6 2.0 %gather_fusion.1 = f32[72,4096]{1,0:T(8,128)} fusion(f32[48,4096]{1,0:T(8,128)S(1)} %bitcast.108, s32[1024]{0:T(1024)S(1)} %pad_clamp_fusion), kind=kCustom, calls=%fused_computation.1 | custom fusion | bytes 2359584 | tf_op jit(solution)/shard_map/jit(_take)/gather | solution.py:120
  140.4 4.3 %all-to-all-start.2 = ((f32[8,32,9,128]{3,1,2,0:T(8,128)}), f32[8,32,9,128]{3,1,2,0:T(8,128)}, u32[]{:S(2)}, u32[]{:S(2)}) async-start(f32[8,32,9,128]{3,1,2,0:T(8,128)} %select_bitcast_fusion), calls=%async_computation.2 | async-start | bytes 2359296 | tf_op jit(solution)/shard_map/all_to_all | solution.py:122
  144.7 3.2 %subtract_convert_fusion.1 = (bf16[16,16,1024]{2,1,0:T(8,128)(2,1)S(1)}, bf16[16,16,1024]{2,1,0:T(8,128)(2,1)S(1)}) fusion(bf16[16,48,16]{1,2,0:T(8,128)(2,1)S(1)} %copy-done.9, bf16[48,16,1024]{2,1,0:T(8,128)(2,1)} %copy-done.1), kind=kOutput, calls=%fused_computation.44 | convolution fusion | flops 26214400 | bytes 2646016 | tf_op jit(solution)/shard_map/tvh,vtd->thd/dot_general | solution.py:41
  148.5 13.6 %all-to-all-done.2 = f32[8,32,9,128]{3,1,2,0:T(8,128)} async-done(((f32[8,32,9,128]{3,1,2,0:T(8,128)}), f32[8,32,9,128]{3,1,2,0:T(8,128)}, u32[]{:S(2)}, u32[]{:S(2)}) %all-to-all-start.2) | async-done | bytes 1179680 | tf_op jit(solution)/shard_map/all_to_all | solution.py:122
  164.3 5.8 %all-to-all-start.3 = ((f32[32,9,128]{2,1,0:T(8,128)}), f32[32,9,128]{2,1,0:T(8,128)S(1)}, u32[]{:S(2)}, u32[]{:S(2)}) async-start(f32[32,9,128]{2,1,0:T(8,128)} %copy.98), calls=%async_computation.3 | async-start | bytes 524288 | tf_op jit(solution)/shard_map/all_to_all | solution.py:123
  170.9 2.6 %fusion.26 = bf16[16,1024]{1,0:T(8,128)(2,1)} fusion(bf16[16,1024]{1,0:T(8,128)(2,1)S(1)} %reshape.73, bf16[2,1024,1024]{2,1,0:T(8,128)(2,1)} %all-gather.2.cloned.1.call-done), kind=kOutput, calls=%fused_computation.40 | convolution fusion | flops 33570816 | bytes 2162688 | tf_op jit(solution)/shard_map/dot_general | solution.py:93
  173.5 8.6 %all-to-all-done.3 = f32[32,9,128]{2,1,0:T(8,128)S(1)} async-done(((f32[32,9,128]{2,1,0:T(8,128)}), f32[32,9,128]{2,1,0:T(8,128)S(1)}, u32[]{:S(2)}, u32[]{:S(2)}) %all-to-all-start.3) | async-done | bytes 147488 | tf_op jit(solution)/shard_map/all_to_all | solution.py:123
  (94 shorter events, 31.7 us)
Async XLA Ops:
  7.2 30.9 %copy-start = (bf16[48,4,1024]{2,1,0:T(4,128)(2,1)S(1)}, bf16[48,4,1024]{2,1,0:T(4,128)(2,1)}, u32[]{:S(2)}) copy-start(bf16[48,4,1024]{2,1,0:T(4,128)(2,1)} %param.11) | copy-start | bytes 1179652
  7.2 87.5 %all-gather.2.cloned.1.call-start = ((), (), s32[]{:S(2)}) async-start(), calls=%async_computation.4 | async-start | bytes 4325376 | tf_op jit(solution)/shard_map/all_gather | solution.py:67
  15.8 10.4 %all-to-all-start.1 = ((bf16[8,2,288]{2,1,0:T(2,128)(2,1)}), bf16[8,2,288]{2,1,0:T(2,128)(2,1)S(1)}, u32[]{:S(2)}, u32[]{:S(2)}) async-start(bf16[8,2,288]{2,1,0:T(2,128)(2,1)} %reshape.97), calls=%async_computation.1 | async-start | bytes 24576 | tf_op jit(solution)/shard_map/all_to_all | solution.py:71
  23.0 18.1 %copy-start.18 = (pred[48]{0:T(512)(128)(4,1)}, pred[48]{0:T(512)(128)(4,1)S(1)}, u32[]{:S(2)}) copy-start(pred[48]{0:T(512)(128)(4,1)S(1)} %compare_and_fusion.1) | copy-start | bytes 148
  24.6 22.9 %copy-start.10 = (f32[48,1024]{1,0:T(8,128)}, f32[48,1024]{1,0:T(8,128)S(1)}, u32[]{:S(2)}) copy-start(f32[48,1024]{1,0:T(8,128)S(1)} %convert_element_type.88) | copy-start | bytes 589828
  26.1 20.9 %all-to-all-start = ((f32[32,1,512]{2,1,0:T(1,128)}), f32[32,1,512]{2,1,0:T(1,128)S(1)}, u32[]{:S(2)}, u32[]{:S(2)}) async-start(f32[32,1,512]{2,1,0:T(1,128)} %reshape.99), calls=%async_computation | async-start | bytes 131072 | tf_op jit(solution)/shard_map/all_to_all | solution.py:65
  38.1 8.9 %copy-start.12 = (bf16[48,4,16]{2,1,0:T(4,128)(2,1)}, bf16[48,4,16]{2,1,0:T(4,128)(2,1)S(1)}, u32[]{:S(2)}) copy-start(bf16[48,4,16]{2,1,0:T(4,128)(2,1)S(1)} %gather_fusion) | copy-start | bytes 18436
  41.1 53.6 %copy-start.1 = (bf16[48,16,1024]{2,1,0:T(8,128)(2,1)}, bf16[48,16,1024]{2,1,0:T(8,128)(2,1)S(1)}, u32[]{:S(2)}) copy-start(bf16[48,16,1024]{2,1,0:T(8,128)(2,1)S(1)} %get-tuple-element.11) | copy-start | bytes 4718596
  48.7 46.0 %copy-start.5 = (f32[1024,16]{0,1:T(8,128)}, f32[1024,16]{0,1:T(8,128)S(1)}, u32[]{:S(2)}) copy-start(f32[1024,16]{0,1:T(8,128)S(1)} %reshape.71) | copy-start | bytes 196612
  52.2 48.7 %copy-start.20 = (bf16[16,1024]{1,0:T(8,128)(2,1)S(1)}, bf16[16,1024]{1,0:T(8,128)(2,1)}, u32[]{:S(2)}) copy-start(bf16[16,1024]{1,0:T(8,128)(2,1)} %param.17) | copy-start | bytes 98308
  105.2 4.2 %copy-start.15 = (f32[16,48,16]{1,0,2:T(8,128)S(1)}, f32[16,48,16]{1,0,2:T(8,128)}, u32[]{:S(2)}) copy-start(f32[16,48,16]{1,0,2:T(8,128)} %copy-done.14) | copy-start | bytes 147460
  113.0 3.3 %copy-start.4 = (bf16[16,48,16]{2,0,1:T(8,128)(2,1)S(1)}, bf16[16,48,16]{2,0,1:T(8,128)(2,1)}, u32[]{:S(2)}) copy-start(bf16[16,48,16]{2,0,1:T(8,128)(2,1)} %copy.95) | copy-start | bytes 73732
  113.0 3.3 %copy-start.6 = (f32[1024,16]{0,1:T(8,128)S(1)}, f32[1024,16]{0,1:T(8,128)}, u32[]{:S(2)}) copy-start(f32[1024,16]{0,1:T(8,128)} %copy-done.5) | copy-start | bytes 196612
  113.0 5.6 %copy-start.8 = (bf16[16,48,16]{1,2,0:T(8,128)(2,1)S(1)}, bf16[16,48,16]{1,2,0:T(8,128)(2,1)}, u32[]{:S(2)}) copy-start(bf16[16,48,16]{1,2,0:T(8,128)(2,1)} %fusion.59) | copy-start | bytes 73732
  120.9 2.3 %copy-start.16 = (bf16[16,48,16]{1,2,0:T(8,128)(2,1)S(1)}, bf16[16,48,16]{1,2,0:T(8,128)(2,1)}, u32[]{:S(2)}) copy-start(bf16[16,48,16]{1,2,0:T(8,128)(2,1)} %get-tuple-element.4) | copy-start | bytes 73732
  120.9 2.5 %copy-start.7 = (f32[1024,16]{0,1:T(8,128)S(1)}, f32[1024,16]{0,1:T(8,128)}, u32[]{:S(2)}) copy-start(f32[1024,16]{0,1:T(8,128)} %copy-done.5) | copy-start | bytes 196612
  123.4 8.5 %copy-start.3 = (f32[48,16,1024]{2,1,0:T(8,128)S(1)}, f32[48,16,1024]{2,1,0:T(8,128)}, u32[]{:S(2)}) copy-start(f32[48,16,1024]{2,1,0:T(8,128)} %get-tuple-element.12) | copy-start | bytes 9437188
  123.4 8.5 %copy-start.11 = (f32[48,1024]{1,0:T(8,128)S(1)}, f32[48,1024]{1,0:T(8,128)}, u32[]{:S(2)}) copy-start(f32[48,1024]{1,0:T(8,128)} %copy-done.10) | copy-start | bytes 589828
  123.4 8.5 %copy-start.13 = (bf16[48,4,16]{2,1,0:T(4,128)(2,1)S(1)}, bf16[48,4,16]{2,1,0:T(4,128)(2,1)}, u32[]{:S(2)}) copy-start(bf16[48,4,16]{2,1,0:T(4,128)(2,1)} %copy-done.12) | copy-start | bytes 18436
  123.4 8.5 %copy-start.19 = (pred[48]{0:T(512)(128)(4,1)S(1)}, pred[48]{0:T(512)(128)(4,1)}, u32[]{:S(2)}) copy-start(pred[48]{0:T(512)(128)(4,1)} %copy-done.18) | copy-start | bytes 148
  135.6 3.5 %copy-start.17 = (pred[8,9]{1,0:T(8,128)(4,1)S(1)}, pred[8,9]{1,0:T(8,128)(4,1)}, u32[]{:S(2)}) copy-start(pred[8,9]{1,0:T(8,128)(4,1)} %broadcast_in_dim.69) | copy-start | bytes 220
  137.6 7.1 %copy-start.9 = (bf16[16,48,16]{1,2,0:T(8,128)(2,1)S(1)}, bf16[16,48,16]{1,2,0:T(8,128)(2,1)}, u32[]{:S(2)}) copy-start(bf16[16,48,16]{1,2,0:T(8,128)(2,1)} %fusion.59) | copy-start | bytes 73732
  140.4 21.7 %all-to-all-start.2 = ((f32[8,32,9,128]{3,1,2,0:T(8,128)}), f32[8,32,9,128]{3,1,2,0:T(8,128)}, u32[]{:S(2)}, u32[]{:S(2)}) async-start(f32[8,32,9,128]{3,1,2,0:T(8,128)} %select_bitcast_fusion), calls=%async_computation.2 | async-start | bytes 2359296 | tf_op jit(solution)/shard_map/all_to_all | solution.py:122
  164.3 17.8 %all-to-all-start.3 = ((f32[32,9,128]{2,1,0:T(8,128)}), f32[32,9,128]{2,1,0:T(8,128)S(1)}, u32[]{:S(2)}, u32[]{:S(2)}) async-start(f32[32,9,128]{2,1,0:T(8,128)} %copy.98), calls=%async_computation.3 | async-start | bytes 524288 | tf_op jit(solution)/shard_map/all_to_all | solution.py:123
  (2 other events, 2.1 us)
Sparse Core Ops, SparseCore 0:
  10.6 84.0 all-gather.1
